TPU v7x, 512 devices: a whole 4x4x16 slice. The times are simulated.
512 devices in a mesh: section: 32 (over z, core), blk: 16 (over y, x).
Axes of the slice: x: 4, y: 4, z: 16, core: 2. Of those that a mesh axis runs over, the one named last changes fastest.
Arguments:
- held_input: bfloat16 [32, 5120, 128], P('section', 'blk'), may hold values from -6 to 6
- fresh_input: bfloat16 [5120, 128], P('blk'), may hold values from -6 to 6
- stashed: bfloat16 [32, 2, 5120, 128], P('section', None, 'blk'), may hold values from -6 to 6
- held_grad: bfloat16 [32, 5120, 128], P('section', 'blk'), may hold values from -6 to 6
- fresh_grad: bfloat16 [5120, 128], P('blk'), may hold values from -6 to 6
- first_up: bfloat16 [32, 2, 128, 6400], P('section', None, 'blk'), may hold values from -1 to 1
- second_up: bfloat16 [32, 2, 160, 16384], P('section', None, 'blk'), may hold values from -0.5 to 0.5
- first_down: bfloat16 [32, 160, 16384], P('section', 'blk'), may hold values from -0.5 to 0.5
- second_down: bfloat16 [32, 128, 6400], P('section', 'blk'), may hold values from -0.5 to 0.5
Outputs:
- passed_output: bfloat16 [32, 5120, 128], P('section', 'blk')
- passed_grad: bfloat16 [32, 5120, 128], P('section', 'blk')
- grad_first_up: bfloat16 [32, 2, 128, 6400], P('section', None, 'blk')
- grad_second_up: bfloat16 [32, 2, 160, 16384], P('section', None, 'blk')
- grad_first_down: bfloat16 [32, 160, 16384], P('section', 'blk')
- grad_second_down: bfloat16 [32, 128, 6400], P('section', 'blk')
All inputs are finite; a program needn't handle non-finite values.
Results may differ from a plain program's by a relative error of at most 0.0095.
Values may be sent and summed in bfloat16 or wider, within the bound.
No kernel may reach another device: no remote copies, remote signals or barrier semaphores. Data moves between devices by JAX's collectives and lax.ppermute only.
A program may use at most 64 MiB of HBM per device.

v0:
```python
import math
import jax
import jax.numpy as jnp
from jax import lax
from jax.sharding import PartitionSpec as P

BLOCK = 128
FIRST_BLOCKS = 128
FIRST_IN = 40
SECOND_BLOCKS = 160
TICKS = 2


def from_behind(value, axis, by):
    length = lax.axis_size(axis)
    pairs = [(i, i + by) for i in range(length) if 0 <= i + by < length]
    return lax.ppermute(value, axis, pairs)


def to_blocks(pieces):
    return lax.all_to_all(pieces, "blk", split_axis=2, concat_axis=1, tiled=True)


def to_features(pieces):
    return lax.all_to_all(pieces, "blk", split_axis=2, concat_axis=1, tiled=True)


def first_half(values, up_first):
    return jnp.einsum(
        "pqt,gpqr->gprt", values, up_first, preferred_element_type=jnp.float32
    ).astype(jnp.bfloat16)


def middle(spread, up_second, down_first):
    mixed = jnp.einsum("gprt,grpo->grot", spread, up_second, preferred_element_type=jnp.float32)
    hidden = (jax.nn.silu(mixed[0]) * mixed[1]).astype(jnp.bfloat16)
    lowered = jnp.einsum(
        "rot,rop->rpt", hidden, down_first, preferred_element_type=jnp.float32
    ).astype(jnp.bfloat16)
    return (mixed, hidden, lowered)


def last_half(values, lowered, down_second):
    added = jnp.einsum("rpt,prq->pqt", lowered, down_second, preferred_element_type=jnp.float32)
    return (values.astype(jnp.float32) + added).astype(jnp.bfloat16)


def backward_middle(mixed, grad_lowered, up_second, down_first):
    grad_hidden = jnp.einsum(
        "prt,rop->rot", grad_lowered, down_first, preferred_element_type=jnp.float32
    )
    sigmoid_gate = jax.nn.sigmoid(mixed[0])
    slope = sigmoid_gate * (1.0 + mixed[0] * (1.0 - sigmoid_gate))
    grad_mixed = jnp.stack(
        [grad_hidden * mixed[1] * slope, grad_hidden * mixed[0] * sigmoid_gate]
    ).astype(jnp.bfloat16)
    grad_spread = jnp.einsum(
        "grot,grpo->grpt", grad_mixed, up_second, preferred_element_type=jnp.float32
    ).astype(jnp.bfloat16)
    return (grad_mixed, grad_spread)


def shards(
    held_input,
    fresh_input,
    stashed,
    held_grad,
    fresh_grad,
    first_up,
    second_up,
    first_down,
    second_down,
):
    feature_blocks = first_up.shape[2]
    hidden_blocks = second_up.shape[2]
    tokens = held_input.shape[2]
    up_first = first_up[0].reshape(2, feature_blocks, FIRST_IN, SECOND_BLOCKS)
    up_second = second_up[0].reshape(2, hidden_blocks, FIRST_BLOCKS, BLOCK)
    down_first = first_down[0].reshape(hidden_blocks, BLOCK, FIRST_BLOCKS)
    down_second = second_down[0].reshape(feature_blocks, SECOND_BLOCKS, FIRST_IN)
    inputs = held_input[0].reshape(feature_blocks, FIRST_IN, tokens)
    grads = held_grad[0].reshape(feature_blocks, FIRST_IN, tokens)
    section_pos = lax.axis_index("section")
    last_section = lax.axis_size("section") - 1
    total_first_up = jnp.zeros(up_first.shape, jnp.float32)
    total_second_up = jnp.zeros(up_second.shape, jnp.float32)
    total_first_down = jnp.zeros(down_first.shape, jnp.float32)
    total_second_down = jnp.zeros(down_second.shape, jnp.float32)
    outputs = inputs
    backward = grads
    for tick_index in range(TICKS):
        stash_view = stashed[0, tick_index].reshape(feature_blocks, FIRST_IN, tokens)
        grad_lowered = jnp.einsum(
            "pqt,prq->prt", grads, down_second, preferred_element_type=jnp.float32
        ).astype(jnp.bfloat16)
        spread = to_blocks(first_half(inputs, up_first))
        mixed, hidden, lowered = middle(spread, up_second, down_first)
        outputs = last_half(inputs, to_features(lowered[None])[0], down_second)
        spread_stash = to_blocks(first_half(stash_view, up_first))
        mixed_stash, hidden_stash, lowered_stash = middle(spread_stash, up_second, down_first)
        lowered_back = to_features(lowered_stash[None])[0]
        grad_arrived = to_blocks(grad_lowered[None])[0]
        grad_mixed, grad_spread = backward_middle(mixed_stash, grad_arrived, up_second, down_first)
        grad_spread_back = to_features(grad_spread)
        added_back = jnp.einsum(
            "grpt,gpqr->pqt", grad_spread_back, up_first, preferred_element_type=jnp.float32
        )
        backward = (grads.astype(jnp.float32) + added_back).astype(jnp.bfloat16)
        total_first_up = total_first_up + jnp.einsum(
            "pqt,grpt->gpqr", stash_view, grad_spread_back, preferred_element_type=jnp.float32
        )
        total_second_up = total_second_up + jnp.einsum(
            "gprt,grot->grpo", spread_stash, grad_mixed, preferred_element_type=jnp.float32
        )
        total_first_down = total_first_down + jnp.einsum(
            "rot,prt->rop", hidden_stash, grad_arrived, preferred_element_type=jnp.float32
        )
        total_second_down = total_second_down + jnp.einsum(
            "rpt,pqt->prq", lowered_back, grads, preferred_element_type=jnp.float32
        )
        if tick_index + 1 < TICKS:
            moved_forward = from_behind(outputs, "section", 1)
            inputs = jnp.where(
                section_pos == 0,
                fresh_input.reshape(feature_blocks, FIRST_IN, tokens),
                moved_forward,
            )
            moved_backward = from_behind(backward, "section", -1)
            grads = jnp.where(
                section_pos == last_section,
                fresh_grad.reshape(feature_blocks, FIRST_IN, tokens),
                moved_backward,
            )
    factor = 1.0 / math.sqrt(TICKS * tokens)
    return (
        outputs.reshape(held_input.shape),
        backward.reshape(held_grad.shape),
        (total_first_up * factor).astype(jnp.bfloat16).reshape(first_up.shape),
        (total_second_up * factor).astype(jnp.bfloat16).reshape(second_up.shape),
        (total_first_down * factor).astype(jnp.bfloat16).reshape(first_down.shape),
        (total_second_down * factor).astype(jnp.bfloat16).reshape(second_down.shape),
    )


def solution(mesh):
    return jax.shard_map(
        shards,
        mesh=mesh,
        in_specs=(
            P("section", "blk", None),
            P("blk", None),
            P("section", None, "blk", None),
            P("section", "blk", None),
            P("blk", None),
            P("section", None, "blk", None),
            P("section", None, "blk", None),
            P("section", "blk", None),
            P("section", "blk", None),
        ),
        out_specs=(
            P("section", "blk", None),
            P("section", "blk", None),
            P("section", None, "blk", None),
            P("section", None, "blk", None),
            P("section", "blk", None),
            P("section", "blk", None),
        ),
        check_vma=False,
    )
```

profile of v0, /device:TPU:224, one launch (start us, length us, event | category | flops | bytes accessed | tf_op | source)
XLA Modules:
  0.0 197.9 jit_solution(12979514578403921260)
XLA Ops:
  0.6 1.4 reshape_squeeze.25
  2.0 1.3 fusion.6
  3.3 1.3 copy.186
  4.7 7.0 %all-to-all-start = ((bf16[2,8,160,128]{3,0,1,2:T(2,128)(2,1)}), bf16[2,8,160,128]{3,0,1,2:T(2,128)(2,1)S(1)}, u32[]{:S(2)}, u32[]{:S(2)}) async-start(bf16[2,8,160,128]{3,0,1,2:T(2,128)(2,1)} %copy.186), calls=%async_computation | async-start | bytes 1310720 | tf_op jit(solution)/shard_map/all_to_all | solution.py:21
  12.2 1.3 copy.212
  13.5 11.1 %all-to-all-done = bf16[2,8,160,128]{3,0,1,2:T(2,128)(2,1)S(1)} async-done(((bf16[2,8,160,128]{3,0,1,2:T(2,128)(2,1)}), bf16[2,8,160,128]{3,0,1,2:T(2,128)(2,1)S(1)}, u32[]{:S(2)}, u32[]{:S(2)}) %all-to-all-start) | async-done | bytes 655392 | tf_op jit(solution)/shard_map/all_to_all | solution.py:21
  24.6 4.3 %all-to-all-start.5 = ((bf16[2,8,160,128]{3,0,1,2:T(2,128)(2,1)}), bf16[2,8,160,128]{3,0,1,2:T(2,128)(2,1)}, u32[]{:S(2)}, u32[]{:S(2)}) async-start(bf16[2,8,160,128]{3,0,1,2:T(2,128)(2,1)} %copy.212), calls=%async_computation.5 | async-start | bytes 1310720 | tf_op jit(solution)/shard_map/all_to_all | solution.py:21
  30.0 1.1 copy.276
  32.6 1.4 copy.228
  34.1 6.6 %all-to-all-done.5 = bf16[2,8,160,128]{3,0,1,2:T(2,128)(2,1)} async-done(((bf16[2,8,160,128]{3,0,1,2:T(2,128)(2,1)}), bf16[2,8,160,128]{3,0,1,2:T(2,128)(2,1)}, u32[]{:S(2)}, u32[]{:S(2)}) %all-to-all-start.5) | async-done | bytes 655392 | tf_op jit(solution)/shard_map/all_to_all | solution.py:21
  40.7 3.5 %all-to-all-start.4 = ((bf16[1,8,160,128]{3,1,0,2:T(8,128)(2,1)}), bf16[1,8,160,128]{3,1,0,2:T(8,128)(2,1)S(1)}, u32[]{:S(2)}, u32[]{:S(2)}) async-start(bf16[1,8,160,128]{3,1,0,2:T(8,128)(2,1)} %copy.208), calls=%async_computation.4 | async-start | bytes 655360 | tf_op jit(solution)/shard_map/all_to_all | solution.py:21
  44.3 1.5 convolution_bitcast_fusion.3
  45.7 1.2 copy.213
  46.9 1.4 convolution_bitcast_fusion.1
  48.4 4.9 %all-to-all-done.4 = bf16[1,8,160,128]{3,1,0,2:T(8,128)(2,1)S(1)} async-done(((bf16[1,8,160,128]{3,1,0,2:T(8,128)(2,1)}), bf16[1,8,160,128]{3,1,0,2:T(8,128)(2,1)S(1)}, u32[]{:S(2)}, u32[]{:S(2)}) %all-to-all-start.4) | async-done | bytes 327712 | tf_op jit(solution)/shard_map/all_to_all | solution.py:21
  54.1 3.6 %all-to-all-start.8 = ((bf16[2,8,160,128]{3,0,1,2:T(2,128)(2,1)}), bf16[2,8,160,128]{3,0,1,2:T(2,128)(2,1)S(1)}, u32[]{:S(2)}, u32[]{:S(2)}) async-start(bf16[2,8,160,128]{3,0,1,2:T(2,128)(2,1)} %copy.228), calls=%async_computation.8 | async-start | bytes 1310720 | tf_op jit(solution)/shard_map/all_to_all | solution.py:21
  57.7 2.3 %fusion.12 = bf16[1,10,128,128]{2,3,1,0:T(8,128)(2,1)} fusion(f32[2,10,128,128]{2,3,1,0:T(8,128)} %convolution_bitcast_fusion.3, bf16[16,128,128]{2,1,0:T(8,128)(2,1)S(1)} %bitcast.294), kind=kOutput, calls=%fused_computation.33 | convolution fusion | flops 43089920 | bytes 1966080 | tf_op jit(solution)/shard_map/rot,rop->rpt/dot_general | solution.py:37
  60.0 2.2 %copy.191 = bf16[1,10,128,128]{3,1,0,2:T(8,128)(2,1)} copy(bf16[1,10,128,128]{2,3,1,0:T(8,128)(2,1)} %fusion.12) | data formatting | bytes 655360 | tf_op jit(solution)/shard_map/broadcast_in_dim | solution.py:98
  62.1 2.7 %fusion.61 = (bf16[1,10,128,128]{2,3,1,0:T(8,128)(2,1)S(1)}, bf16[1,10,128,128]{2,3,1,0:T(8,128)(2,1)S(1)}, bf16[10,128,128]{1,2,0:T(8,128)(2,1)}) fusion(f32[2,10,128,128]{2,3,1,0:T(8,128)} %convolution_bitcast_fusion.1, bf16[16,128,128]{2,1,0:T(8,128)(2,1)S(1)} %bitcast.295, bf16[1,16,8,10,128]{4,2,3,1,0:T(8,128)(2,1)} %bitcast.308), kind=kOutput, calls=%fused_computation.109 | convolution fusion | flops 44564480 | bytes 2949120 | tf_op jit(solution)/shard_map/prt,rop->rot/dot_general | solution.py:49
  65.6 1.4 fusion.2
  67.1 1.4 all-to-all-done.8
  68.5 5.8 %all-to-all-start.1 = ((bf16[1,10,128,128]{3,1,0,2:T(8,128)(2,1)}), bf16[1,10,128,128]{3,1,0,2:T(8,128)(2,1)}, u32[]{:S(2)}, u32[]{:S(2)}) async-start(bf16[1,10,128,128]{3,1,0,2:T(8,128)(2,1)} %copy.191), calls=%async_computation.1 | async-start | bytes 1048576 | tf_op jit(solution)/shard_map/all_to_all | solution.py:25
  74.3 1.9 fusion.14
  76.2 2.2 %copy.246 = bf16[1,10,128,128]{3,1,0,2:T(8,128)(2,1)} copy(bf16[1,10,128,128]{2,3,1,0:T(8,128)(2,1)} %fusion.14) | data formatting | bytes 655360 | tf_op jit(solution)/shard_map/broadcast_in_dim | solution.py:101
  78.4 1.4 fusion.31
  79.8 4.7 %all-to-all-done.1 = bf16[1,10,128,128]{3,1,0,2:T(8,128)(2,1)} async-done(((bf16[1,10,128,128]{3,1,0,2:T(8,128)(2,1)}), bf16[1,10,128,128]{3,1,0,2:T(8,128)(2,1)}, u32[]{:S(2)}, u32[]{:S(2)}) %all-to-all-start.1) | async-done | bytes 327712 | tf_op jit(solution)/shard_map/all_to_all | solution.py:25
  84.5 4.2 %all-to-all-start.10 = ((bf16[1,10,128,128]{3,1,0,2:T(8,128)(2,1)}), bf16[1,10,128,128]{3,1,0,2:T(8,128)(2,1)}, u32[]{:S(2)}, u32[]{:S(2)}) async-start(bf16[1,10,128,128]{3,1,0,2:T(8,128)(2,1)} %copy.246), calls=%async_computation.10 | async-start | bytes 1048576 | tf_op jit(solution)/shard_map/all_to_all | solution.py:25
  88.7 2.3 %fusion.49 = f32[10,128,128]{2,1,0:T(8,128)} fusion(bf16[10,128,128]{1,2,0:T(8,128)(2,1)} %get-tuple-element.35, bf16[1,16,8,10,128]{4,2,3,1,0:T(8,128)(2,1)} %bitcast.309), kind=kOutput, calls=%fused_computation.95 | convolution fusion | flops 41943040 | bytes 1310720 | tf_op jit(solution)/shard_map/rot,prt->rop/dot_general | solution.py:115
  91.0 1.9 copy.218
  92.9 1.2 copy.229
  94.1 1.5 convolution_bitcast_fusion
  95.6 1.2 copy.378
  97.5 1.4 all-to-all-done.10
  98.9 5.8 %all-to-all-start.6 = ((bf16[2,10,128,128]{3,0,1,2:T(2,128)(2,1)}), bf16[2,10,128,128]{3,0,1,2:T(2,128)(2,1)}, u32[]{:S(2)}, u32[]{:S(2)}) async-start(bf16[2,10,128,128]{3,0,1,2:T(2,128)(2,1)} %copy.218), calls=%async_computation.6 | async-start | bytes 1310720 | tf_op jit(solution)/shard_map/all_to_all | solution.py:25
  104.7 1.3 fusion.24
  106.0 2.2 %collective-permute-start = (bf16[8,40,128]{2,1,0:T(8,128)(2,1)S(1)}, bf16[8,40,128]{2,1,0:T(8,128)(2,1)S(1)}, u32[]{:S(2)}, u32[]{:S(2)}) collective-permute-start(bf16[8,40,128]{2,1,0:T(8,128)(2,1)S(1)} %fusion.24), channel_id=1, source_target_pairs={{0,16},{16,32},{32,48},{48,64},{64,80},{80,96},{96,112},{112,128},... | collective-permute-start | bytes 245768 | tf_op jit(solution)/shard_map/ppermute | solution.py:17
  108.2 1.1 copy.376
  109.4 1.1 fusion.53
  110.5 1.4 collective-permute-done
  112.9 1.3 copy.197
  114.3 1.3 all-to-all-done.6
  115.6 5.9 %all-to-all-start.2 = ((bf16[2,8,160,128]{3,0,1,2:T(2,128)(2,1)}), bf16[2,8,160,128]{3,0,1,2:T(2,128)(2,1)}, u32[]{:S(2)}, u32[]{:S(2)}) async-start(bf16[2,8,160,128]{3,0,1,2:T(2,128)(2,1)} %copy.197), calls=%async_computation.2 | async-start | bytes 1310720 | tf_op jit(solution)/shard_map/all_to_all | solution.py:21
  121.5 1.2 copy.374
  123.2 2.0 %collective-permute-start.1 = (bf16[8,40,128]{2,1,0:T(8,128)(2,1)S(1)}, bf16[8,40,128]{2,1,0:T(8,128)(2,1)S(1)}, u32[]{:S(2)}, u32[]{:S(2)}) collective-permute-start(bf16[8,40,128]{2,1,0:T(8,128)(2,1)S(1)} %fusion.23), channel_id=1, source_target_pairs={{16,0},{32,16},{48,32},{64,48},{80,64},{96,80},{112,96},{128,112},... | collective-permute-start | bytes 245768 | tf_op jit(solution)/shard_map/ppermute | solution.py:17
  125.2 1.4 fusion.42
  128.6 6.7 %all-to-all-done.2 = bf16[2,8,160,128]{3,0,1,2:T(2,128)(2,1)} async-done(((bf16[2,8,160,128]{3,0,1,2:T(2,128)(2,1)}), bf16[2,8,160,128]{3,0,1,2:T(2,128)(2,1)}, u32[]{:S(2)}, u32[]{:S(2)}) %all-to-all-start.2) | async-done | bytes 655392 | tf_op jit(solution)/shard_map/all_to_all | solution.py:21
  135.3 4.2 %all-to-all-start.7 = ((bf16[1,8,160,128]{3,1,0,2:T(8,128)(2,1)}), bf16[1,8,160,128]{3,1,0,2:T(8,128)(2,1)}, u32[]{:S(2)}, u32[]{:S(2)}) async-start(bf16[1,8,160,128]{3,1,0,2:T(8,128)(2,1)} %copy.224), calls=%async_computation.7 | async-start | bytes 655360 | tf_op jit(solution)/shard_map/all_to_all | solution.py:21
  139.5 1.2 copy.198
  142.8 2.2 %copy.202 = bf16[1,10,128,128]{3,1,0,2:T(8,128)(2,1)} copy(bf16[1,10,128,128]{2,3,1,0:T(8,128)(2,1)} %fusion.13) | data formatting | bytes 655360 | tf_op jit(solution)/shard_map/broadcast_in_dim | solution.py:98
  144.9 4.9 %all-to-all-done.7 = bf16[1,8,160,128]{3,1,0,2:T(8,128)(2,1)} async-done(((bf16[1,8,160,128]{3,1,0,2:T(8,128)(2,1)}), bf16[1,8,160,128]{3,1,0,2:T(8,128)(2,1)}, u32[]{:S(2)}, u32[]{:S(2)}) %all-to-all-start.7) | async-done | bytes 327712 | tf_op jit(solution)/shard_map/all_to_all | solution.py:21
  149.8 4.2 %all-to-all-start.3 = ((bf16[1,10,128,128]{3,1,0,2:T(8,128)(2,1)}), bf16[1,10,128,128]{3,1,0,2:T(8,128)(2,1)}, u32[]{:S(2)}, u32[]{:S(2)}) async-start(bf16[1,10,128,128]{3,1,0,2:T(8,128)(2,1)} %copy.202), calls=%async_computation.3 | async-start | bytes 1048576 | tf_op jit(solution)/shard_map/all_to_all | solution.py:25
  154.1 3.0 %fusion.62 = (bf16[1,10,128,128]{2,3,1,0:T(8,128)(2,1)}, bf16[1,10,128,128]{2,3,1,0:T(8,128)(2,1)}, bf16[10,128,128]{1,2,0:T(8,128)(2,1)S(1)}) fusion(f32[2,10,128,128]{2,3,1,0:T(8,128)} %convolution_bitcast_fusion, bf16[16,128,128]{2,1,0:T(8,128)(2,1)} %bitcast.297, bf16[1,16,8,10,128]{4,2,3,1,0:T(8,128)(2,1)} %bitcast.62), kind=kOutput, calls=%fused_computation.110 | convolution fusion | flops 44564480 | bytes 2949120 | tf_op jit(solution)/shard_map/prt,rop->rot/dot_general | solution.py:49
  158.7 2.2 %copy.250 = bf16[1,10,128,128]{3,1,0,2:T(8,128)(2,1)} copy(bf16[1,10,128,128]{2,3,1,0:T(8,128)(2,1)} %fusion.15) | data formatting | bytes 655360 | tf_op jit(solution)/shard_map/broadcast_in_dim | solution.py:101
  160.9 4.5 %all-to-all-done.3 = bf16[1,10,128,128]{3,1,0,2:T(8,128)(2,1)} async-done(((bf16[1,10,128,128]{3,1,0,2:T(8,128)(2,1)}), bf16[1,10,128,128]{3,1,0,2:T(8,128)(2,1)}, u32[]{:S(2)}, u32[]{:S(2)}) %all-to-all-start.3) | async-done | bytes 327712 | tf_op jit(solution)/shard_map/all_to_all | solution.py:25
  165.4 4.2 %all-to-all-start.11 = ((bf16[1,10,128,128]{3,1,0,2:T(8,128)(2,1)}), bf16[1,10,128,128]{3,1,0,2:T(8,128)(2,1)}, u32[]{:S(2)}, u32[]{:S(2)}) async-start(bf16[1,10,128,128]{3,1,0,2:T(8,128)(2,1)} %copy.250), calls=%async_computation.11 | async-start | bytes 1048576 | tf_op jit(solution)/shard_map/all_to_all | solution.py:25
  169.6 2.5 %fusion.3 = bf16[2,10,128,128]{2,3,1,0:T(8,128)(2,1)} fusion(bf16[1,10,128,128]{2,3,1,0:T(8,128)(2,1)} %get-tuple-element.31, bf16[1,10,128,128]{2,3,1,0:T(8,128)(2,1)} %get-tuple-element.30, bf16[2,10,128,128]{3,2,0,1:T(8,128)(2,1)S(1)} %reshape_squeeze.26), kind=kOutput, calls=%fused_computation.14 | convolution fusion | flops 84541440 | bytes 1966080 | tf_op jit(solution)/shard_map/grot,grpo->grpt/dot_general | solution.py:57
  172.1 3.0 %copy.234 = bf16[2,10,128,128]{3,0,1,2:T(2,128)(2,1)} copy(bf16[2,10,128,128]{2,3,1,0:T(8,128)(2,1)} %fusion.3) | data formatting | bytes 1310720 | tf_op jit(solution)/shard_map/convert_element_type | solution.py:59
  175.2 1.2 fusion.1
  176.3 3.8 %all-to-all-done.11 = bf16[1,10,128,128]{3,1,0,2:T(8,128)(2,1)} async-done(((bf16[1,10,128,128]{3,1,0,2:T(8,128)(2,1)}), bf16[1,10,128,128]{3,1,0,2:T(8,128)(2,1)}, u32[]{:S(2)}, u32[]{:S(2)}) %all-to-all-start.11) | async-done | bytes 327712 | tf_op jit(solution)/shard_map/all_to_all | solution.py:25
  180.1 3.6 %all-to-all-start.9 = ((bf16[2,10,128,128]{3,0,1,2:T(2,128)(2,1)}), bf16[2,10,128,128]{3,0,1,2:T(2,128)(2,1)S(1)}, u32[]{:S(2)}, u32[]{:S(2)}) async-start(bf16[2,10,128,128]{3,0,1,2:T(2,128)(2,1)} %copy.234), calls=%async_computation.9 | async-start | bytes 1310720 | tf_op jit(solution)/shard_map/all_to_all | solution.py:25
  183.7 1.4 fusion.10
  187.2 1.2 copy.377
  188.5 1.1 copy.375
  192.2 2.7 %all-to-all-done.9 = bf16[2,10,128,128]{3,0,1,2:T(2,128)(2,1)S(1)} async-done(((bf16[2,10,128,128]{3,0,1,2:T(2,128)(2,1)}), bf16[2,10,128,128]{3,0,1,2:T(2,128)(2,1)S(1)}, u32[]{:S(2)}, u32[]{:S(2)}) %all-to-all-start.9) | async-done | bytes 655392 | tf_op jit(solution)/shard_map/all_to_all | solution.py:25
  (87 shorter events, 20.3 us)
Async XLA Ops:
  3.3 8.4 %copy-start.23 = (bf16[1,2,320,128]{3,2,1,0:T(8,128)(2,1)S(1)}, bf16[1,2,320,128]{3,2,1,0:T(8,128)(2,1)}, u32[]{:S(2)}) copy-start(bf16[1,2,320,128]{3,2,1,0:T(8,128)(2,1)} %param.11) | copy-start | bytes 491524
  4.7 20.0 %all-to-all-start = ((bf16[2,8,160,128]{3,0,1,2:T(2,128)(2,1)}), bf16[2,8,160,128]{3,0,1,2:T(2,128)(2,1)S(1)}, u32[]{:S(2)}, u32[]{:S(2)}) async-start(bf16[2,8,160,128]{3,0,1,2:T(2,128)(2,1)} %copy.186), calls=%async_computation | async-start | bytes 1310720 | tf_op jit(solution)/shard_map/all_to_all | solution.py:21
  12.2 16.8 %copy-start.24 = (bf16[1,8,6400]{2,1,0:T(8,128)(2,1)S(1)}, bf16[1,8,6400]{2,1,0:T(8,128)(2,1)}, u32[]{:S(2)}) copy-start(bf16[1,8,6400]{2,1,0:T(8,128)(2,1)} %param.17) | copy-start | bytes 307204
  12.2 17.3 %copy-start.10 = (bf16[1,2,10,16384]{3,1,2,0:T(2,128)(2,1)S(1)}, bf16[1,2,10,16384]{3,1,2,0:T(2,128)(2,1)}, u32[]{:S(2)}) copy-start(bf16[1,2,10,16384]{3,1,2,0:T(2,128)(2,1)} %param.15) | copy-start | bytes 1966084
  24.6 16.1 %all-to-all-start.5 = ((bf16[2,8,160,128]{3,0,1,2:T(2,128)(2,1)}), bf16[2,8,160,128]{3,0,1,2:T(2,128)(2,1)}, u32[]{:S(2)}, u32[]{:S(2)}) async-start(bf16[2,8,160,128]{3,0,1,2:T(2,128)(2,1)} %copy.212), calls=%async_computation.5 | async-start | bytes 1310720 | tf_op jit(solution)/shard_map/all_to_all | solution.py:21
  28.9 2.2 %copy-start.20 = (bf16[1,320,128]{2,1,0:T(8,128)(2,1)S(1)}, bf16[1,320,128]{2,1,0:T(8,128)(2,1)}, u32[]{:S(2)}) copy-start(bf16[1,320,128]{2,1,0:T(8,128)(2,1)} %param.12) | copy-start | bytes 245764
  31.1 43.1 %copy-start = (bf16[2,8,128,128]{3,2,1,0:T(8,128)(2,1)}, bf16[2,8,128,128]{3,2,1,0:T(8,128)(2,1)S(1)}, u32[]{:S(2)}) copy-start(bf16[2,8,128,128]{3,2,1,0:T(8,128)(2,1)S(1)} %copy.276) | copy-start | bytes 1572868
  40.7 12.6 %all-to-all-start.4 = ((bf16[1,8,160,128]{3,1,0,2:T(8,128)(2,1)}), bf16[1,8,160,128]{3,1,0,2:T(8,128)(2,1)S(1)}, u32[]{:S(2)}, u32[]{:S(2)}) async-start(bf16[1,8,160,128]{3,1,0,2:T(8,128)(2,1)} %copy.208), calls=%async_computation.4 | async-start | bytes 655360 | tf_op jit(solution)/shard_map/all_to_all | solution.py:21
  53.3 0.8 copy-start.8
  54.1 14.4 %all-to-all-start.8 = ((bf16[2,8,160,128]{3,0,1,2:T(2,128)(2,1)}), bf16[2,8,160,128]{3,0,1,2:T(2,128)(2,1)S(1)}, u32[]{:S(2)}, u32[]{:S(2)}) async-start(bf16[2,8,160,128]{3,0,1,2:T(2,128)(2,1)} %copy.228), calls=%async_computation.8 | async-start | bytes 1310720 | tf_op jit(solution)/shard_map/all_to_all | solution.py:21
  64.8 0.7 copy-start.18
  64.8 0.8 copy-start.19
  68.5 7.8 %copy-start.5 = (bf16[2,8,160,128]{3,0,1,2:T(2,128)(2,1)}, bf16[2,8,160,128]{3,0,1,2:T(2,128)(2,1)S(1)}, u32[]{:S(2)}) copy-start(bf16[2,8,160,128]{3,0,1,2:T(2,128)(2,1)S(1)} %all-to-all-done.8) | copy-start | bytes 1966084
  68.5 16.0 %all-to-all-start.1 = ((bf16[1,10,128,128]{3,1,0,2:T(8,128)(2,1)}), bf16[1,10,128,128]{3,1,0,2:T(8,128)(2,1)}, u32[]{:S(2)}, u32[]{:S(2)}) async-start(bf16[1,10,128,128]{3,1,0,2:T(8,128)(2,1)} %copy.191), calls=%async_computation.1 | async-start | bytes 1048576 | tf_op jit(solution)/shard_map/all_to_all | solution.py:25
  79.8 11.3 %copy-start.11 = (bf16[2,10,128,128]{2,3,1,0:T(8,128)(2,1)S(1)}, bf16[2,10,128,128]{2,3,1,0:T(8,128)(2,1)}, u32[]{:S(2)}) copy-start(bf16[2,10,128,128]{2,3,1,0:T(8,128)(2,1)} %fusion.2) | copy-start | bytes 1966084
  84.5 14.4 %all-to-all-start.10 = ((bf16[1,10,128,128]{3,1,0,2:T(8,128)(2,1)}), bf16[1,10,128,128]{3,1,0,2:T(8,128)(2,1)}, u32[]{:S(2)}, u32[]{:S(2)}) async-start(bf16[1,10,128,128]{3,1,0,2:T(8,128)(2,1)} %copy.246), calls=%async_computation.10 | async-start | bytes 1048576 | tf_op jit(solution)/shard_map/all_to_all | solution.py:25
  95.6 9.1 %copy-start.12 = (bf16[1,320,128]{2,1,0:T(8,128)(2,1)S(1)}, bf16[1,320,128]{2,1,0:T(8,128)(2,1)}, u32[]{:S(2)}) copy-start(bf16[1,320,128]{2,1,0:T(8,128)(2,1)} %param.9) | copy-start | bytes 245764
  98.9 16.7 %all-to-all-start.6 = ((bf16[2,10,128,128]{3,0,1,2:T(2,128)(2,1)}), bf16[2,10,128,128]{3,0,1,2:T(2,128)(2,1)}, u32[]{:S(2)}, u32[]{:S(2)}) async-start(bf16[2,10,128,128]{3,0,1,2:T(2,128)(2,1)} %copy.218), calls=%async_computation.6 | async-start | bytes 1310720 | tf_op jit(solution)/shard_map/all_to_all | solution.py:25
  104.7 4.8 %copy-start.21 = (bf16[1,320,128]{2,1,0:T(8,128)(2,1)S(1)}, bf16[1,320,128]{2,1,0:T(8,128)(2,1)}, u32[]{:S(2)}) copy-start(bf16[1,320,128]{2,1,0:T(8,128)(2,1)} %param.12) | copy-start | bytes 245764
  106.0 6.5 %copy-start.13 = (bf16[320,128]{1,0:T(8,128)(2,1)S(1)}, bf16[320,128]{1,0:T(8,128)(2,1)}, u32[]{:S(2)}) copy-start(bf16[320,128]{1,0:T(8,128)(2,1)} %param.10) | copy-start | bytes 245764
  106.0 5.9 %collective-permute-start = (bf16[8,40,128]{2,1,0:T(8,128)(2,1)S(1)}, bf16[8,40,128]{2,1,0:T(8,128)(2,1)S(1)}, u32[]{:S(2)}, u32[]{:S(2)}) collective-permute-start(bf16[8,40,128]{2,1,0:T(8,128)(2,1)S(1)} %fusion.24), channel_id=1, source_target_pairs={{0,16},{16,32},{32,48},{48,64},{64,80},{80,96},{96,112},{112,128},... | collective-permute-start | bytes 245768 | tf_op jit(solution)/shard_map/ppermute | solution.py:17
  111.9 0.6 copy-start.14
  115.6 19.8 %all-to-all-start.2 = ((bf16[2,8,160,128]{3,0,1,2:T(2,128)(2,1)}), bf16[2,8,160,128]{3,0,1,2:T(2,128)(2,1)}, u32[]{:S(2)}, u32[]{:S(2)}) async-start(bf16[2,8,160,128]{3,0,1,2:T(2,128)(2,1)} %copy.197), calls=%async_computation.2 | async-start | bytes 1310720 | tf_op jit(solution)/shard_map/all_to_all | solution.py:21
  121.5 1.4 copy-start.22
  122.9 4.6 %copy-start.25 = (bf16[320,128]{1,0:T(8,128)(2,1)S(1)}, bf16[320,128]{1,0:T(8,128)(2,1)}, u32[]{:S(2)}) copy-start(bf16[320,128]{1,0:T(8,128)(2,1)} %param.13) | copy-start | bytes 245764
  123.2 4.3 %collective-permute-start.1 = (bf16[8,40,128]{2,1,0:T(8,128)(2,1)S(1)}, bf16[8,40,128]{2,1,0:T(8,128)(2,1)S(1)}, u32[]{:S(2)}, u32[]{:S(2)}) collective-permute-start(bf16[8,40,128]{2,1,0:T(8,128)(2,1)S(1)} %fusion.23), channel_id=1, source_target_pairs={{16,0},{32,16},{48,32},{64,48},{80,64},{96,80},{112,96},{128,112},... | collective-permute-start | bytes 245768 | tf_op jit(solution)/shard_map/ppermute | solution.py:17
  135.3 14.5 %all-to-all-start.7 = ((bf16[1,8,160,128]{3,1,0,2:T(8,128)(2,1)}), bf16[1,8,160,128]{3,1,0,2:T(8,128)(2,1)}, u32[]{:S(2)}, u32[]{:S(2)}) async-start(bf16[1,8,160,128]{3,1,0,2:T(8,128)(2,1)} %copy.224), calls=%async_computation.7 | async-start | bytes 655360 | tf_op jit(solution)/shard_map/all_to_all | solution.py:21
  140.7 1.0 copy-start.1
  149.8 15.6 %all-to-all-start.3 = ((bf16[1,10,128,128]{3,1,0,2:T(8,128)(2,1)}), bf16[1,10,128,128]{3,1,0,2:T(8,128)(2,1)}, u32[]{:S(2)}, u32[]{:S(2)}) async-start(bf16[1,10,128,128]{3,1,0,2:T(8,128)(2,1)} %copy.202), calls=%async_computation.3 | async-start | bytes 1048576 | tf_op jit(solution)/shard_map/all_to_all | solution.py:25
  154.0 3.7 %copy-start.2 = (bf16[2,8,128,128]{3,2,1,0:T(8,128)(2,1)S(1)}, bf16[2,8,128,128]{3,2,1,0:T(8,128)(2,1)}, u32[]{:S(2)}) copy-start(bf16[2,8,128,128]{3,2,1,0:T(8,128)(2,1)} %copy-done) | copy-start | bytes 1572868
  157.0 0.7 copy-start.9
  165.4 14.8 %all-to-all-start.11 = ((bf16[1,10,128,128]{3,1,0,2:T(8,128)(2,1)}), bf16[1,10,128,128]{3,1,0,2:T(8,128)(2,1)}, u32[]{:S(2)}, u32[]{:S(2)}) async-start(bf16[1,10,128,128]{3,1,0,2:T(8,128)(2,1)} %copy.250), calls=%async_computation.11 | async-start | bytes 1048576 | tf_op jit(solution)/shard_map/all_to_all | solution.py:25
  172.1 3.0 %copy-start.16 = (bf16[1,10,128,128]{2,3,1,0:T(8,128)(2,1)S(1)}, bf16[1,10,128,128]{2,3,1,0:T(8,128)(2,1)}, u32[]{:S(2)}) copy-start(bf16[1,10,128,128]{2,3,1,0:T(8,128)(2,1)} %get-tuple-element.30) | copy-start | bytes 983044
  172.1 3.0 %copy-start.17 = (bf16[1,10,128,128]{2,3,1,0:T(8,128)(2,1)S(1)}, bf16[1,10,128,128]{2,3,1,0:T(8,128)(2,1)}, u32[]{:S(2)}) copy-start(bf16[1,10,128,128]{2,3,1,0:T(8,128)(2,1)} %get-tuple-element.31) | copy-start | bytes 983044
  176.3 7.4 %copy-start.3 = (f32[10,128,128]{2,1,0:T(8,128)S(1)}, f32[10,128,128]{2,1,0:T(8,128)}, u32[]{:S(2)}) copy-start(f32[10,128,128]{2,1,0:T(8,128)} %fusion.49) | copy-start | bytes 1966084
  176.3 8.9 %copy-start.6 = (bf16[2,10,128,128]{3,2,1,0:T(8,128)(2,1)S(1)}, bf16[2,10,128,128]{3,2,1,0:T(8,128)(2,1)}, u32[]{:S(2)}) copy-start(bf16[2,10,128,128]{3,2,1,0:T(8,128)(2,1)} %fusion.1) | copy-start | bytes 1966084
  180.1 14.8 %all-to-all-start.9 = ((bf16[2,10,128,128]{3,0,1,2:T(2,128)(2,1)}), bf16[2,10,128,128]{3,0,1,2:T(2,128)(2,1)S(1)}, u32[]{:S(2)}, u32[]{:S(2)}) async-start(bf16[2,10,128,128]{3,0,1,2:T(2,128)(2,1)} %copy.234), calls=%async_computation.9 | async-start | bytes 1310720 | tf_op jit(solution)/shard_map/all_to_all | solution.py:25
  187.2 2.5 %copy-start.7 = (f32[8,160,40]{1,2,0:T(8,128)S(1)}, f32[8,160,40]{1,2,0:T(8,128)}, u32[]{:S(2)}) copy-start(f32[8,160,40]{1,2,0:T(8,128)} %fusion.53) | copy-start | bytes 614404
  189.6 1.7 copy-start.15
  195.0 1.1 copy-start.4
where the time goes:
time: 200 us; the launch traced here: 198 us
  starting transfers between devices  60.7 us (30%)
  waiting for transfers between devices  56.3 us (28%)
  local copies, waits for them, and re-layouts  43.1 us (22%)
  matrix products  36.6 us (18%)
    all_to_all x6, waiting for transfers between devices, to_blocks(): lax.all_to_all(pieces, 'blk', split_axis=2, concat_axis=1, tiled=True)  35.6 us
    all_to_all x6, starting transfers between devices, to_blocks(): lax.all_to_all(pieces, 'blk', split_axis=2, concat_axis=1, tiled=True)  28.5 us
    all_to_all x6, starting transfers between devices, to_features(): lax.all_to_all(pieces, 'blk', split_axis=2, concat_axis=1, tiled=True)  27.9 us
    all_to_all x6, waiting for transfers between devices, to_features(): lax.all_to_all(pieces, 'blk', split_axis=2, concat_axis=1, tiled=True)  18.3 us
    all_to_all x12, local copies, waits for them, and re-layouts, to_features(): lax.all_to_all(pieces, 'blk', split_axis=2, concat_axis=1, tiled=True)  7.15 us
    dot_general x4, matrix products, middle(): jnp.einsum('rot,rop->rpt', hidden, down_first, preferred_element_type=jnp...  6.25 us
    dot_general x2, matrix products, backward_middle(): jnp.einsum('prt,rop->rot', grad_lowered, down_first, preferred_element_ty...  5.63 us
    unnamed x54, local copies, waits for them, and re-layouts  5.53 us
  transfers between devices with their start and end apart: 14, of which 14 were waited for; matrix products, arithmetic and copies ran while one was open for 35% of the time, Pallas kernels for 0%

commit v1 on v0

--- a/solution.py
+++ b/solution.py
@@ -11,6 +11,14 @@
 TICKS = 2
 
 
+def counts_replace(inp, peer_axis="blk"):
+    ready = jnp.concatenate(
+        lax.all_to_all(jnp.stack(jnp.split(inp, lax.psum(1, peer_axis), axis=2)), peer_axis, 0, 0),
+        axis=1,
+    )
+    return ready
+
+
 def from_behind(value, axis, by):
     length = lax.axis_size(axis)
     pairs = [(i, i + by) for i in range(length) if 0 <= i + by < length]
@@ -22,7 +30,7 @@
 
 
 def to_features(pieces):
-    return lax.all_to_all(pieces, "blk", split_axis=2, concat_axis=1, tiled=True)
+    return counts_replace(pieces)
 
 
 def first_half(values, up_first):

time: 200 us -> 205 us (1.025)
  the two profiles are of different devices: /device:TPU:224 before, /device:TPU:96 now
where the time goes in v1:
time: 205 us; the launch traced here: 203 us
  starting transfers between devices  63.4 us (31%)
  local copies, waits for them, and re-layouts  55.8 us (27%)
  waiting for transfers between devices  51.6 us (25%)
  matrix products  30.4 us (15%)
    unnamed x148, local copies, waits for them, and re-layouts  32.9 us
    all_to_all x6, starting transfers between devices, counts_replace(): lax.all_to_all(jnp.stack(jnp.split(inp, lax.psum(1, peer_axis), axis=2)),...  30.6 us
    all_to_all x6, starting transfers between devices, to_blocks(): lax.all_to_all(pieces, 'blk', split_axis=2, concat_axis=1, tiled=True)  29 us
    all_to_all x6, waiting for transfers between devices, counts_replace(): lax.all_to_all(jnp.stack(jnp.split(inp, lax.psum(1, peer_axis), axis=2)),...  26.1 us
    all_to_all x6, waiting for transfers between devices, to_blocks(): lax.all_to_all(pieces, 'blk', split_axis=2, concat_axis=1, tiled=True)  23.1 us
    convert_element_type x4, local copies, waits for them, and re-layouts, first_half(): return jnp.einsum('pqt,gpqr->gprt', values, up_first, preferred_element_t...  5.42 us
    another operation x6, local copies, waits for them, and re-layouts, counts_replace(): jnp.stack(jnp.split(inp, lax.psum(1, peer_axis), axis=2))  4.74 us
  transfers between devices with their start and end apart: 14, of which 12 were waited for; matrix products, arithmetic and copies ran while one was open for 37% of the time, Pallas kernels for 0%

profile of v1, /device:TPU:96, one launch (start us, length us, event | category | flops | bytes accessed | tf_op | source)
XLA Modules:
  0.0 202.7 jit_solution(2331002262014538120)
XLA Ops:
  0.6 1.4 reshape_squeeze.25
  2.0 1.3 fusion.6
  3.3 1.3 copy.123
  4.7 7.2 %all-to-all-start = ((bf16[2,8,160,128]{3,0,1,2:T(2,128)(2,1)}), bf16[2,8,160,128]{3,0,1,2:T(2,128)(2,1)S(1)}, u32[]{:S(2)}, u32[]{:S(2)}) async-start(bf16[2,8,160,128]{3,0,1,2:T(2,128)(2,1)} %copy.123), calls=%async_computation | async-start | bytes 1310720 | tf_op jit(solution)/shard_map/all_to_all | solution.py:29
  13.1 1.2 fusion.96
  14.6 1.4 copy.147
  16.2 0.9 copy.143
  17.5 1.4 copy.162
  18.9 5.9 %all-to-all-done = bf16[2,8,160,128]{3,0,1,2:T(2,128)(2,1)S(1)} async-done(((bf16[2,8,160,128]{3,0,1,2:T(2,128)(2,1)}), bf16[2,8,160,128]{3,0,1,2:T(2,128)(2,1)S(1)}, u32[]{:S(2)}, u32[]{:S(2)}) %all-to-all-start) | async-done | bytes 655392 | tf_op jit(solution)/shard_map/all_to_all | solution.py:29
  24.8 3.6 %all-to-all-start.5 = ((bf16[2,8,160,128]{3,0,1,2:T(2,128)(2,1)}), bf16[2,8,160,128]{3,0,1,2:T(2,128)(2,1)S(1)}, u32[]{:S(2)}, u32[]{:S(2)}) async-start(bf16[2,8,160,128]{3,0,1,2:T(2,128)(2,1)} %copy.147), calls=%async_computation.5 | async-start | bytes 1310720 | tf_op jit(solution)/shard_map/all_to_all | solution.py:29
  38.4 2.1 %all-to-all-done.5 = bf16[2,8,160,128]{3,0,1,2:T(2,128)(2,1)S(1)} async-done(((bf16[2,8,160,128]{3,0,1,2:T(2,128)(2,1)}), bf16[2,8,160,128]{3,0,1,2:T(2,128)(2,1)S(1)}, u32[]{:S(2)}, u32[]{:S(2)}) %all-to-all-start.5) | async-done | bytes 655392 | tf_op jit(solution)/shard_map/all_to_all | solution.py:29
  40.5 5.1 %all-to-all-start.4 = ((bf16[1,8,160,128]{3,1,0,2:T(8,128)(2,1)}), bf16[1,8,160,128]{3,1,0,2:T(8,128)(2,1)}, u32[]{:S(2)}, u32[]{:S(2)}) async-start(bf16[1,8,160,128]{3,1,0,2:T(8,128)(2,1)} %copy.143), calls=%async_computation.4 | async-start | bytes 655360 | tf_op jit(solution)/shard_map/all_to_all | solution.py:29
  46.3 1.5 convolution_bitcast_fusion.1
  47.8 6.9 %all-to-all-done.4 = bf16[1,8,160,128]{3,1,0,2:T(8,128)(2,1)} async-done(((bf16[1,8,160,128]{3,1,0,2:T(8,128)(2,1)}), bf16[1,8,160,128]{3,1,0,2:T(8,128)(2,1)}, u32[]{:S(2)}, u32[]{:S(2)}) %all-to-all-start.4) | async-done | bytes 327712 | tf_op jit(solution)/shard_map/all_to_all | solution.py:29
  54.7 3.6 %all-to-all-start.8 = ((bf16[2,8,160,128]{3,0,1,2:T(2,128)(2,1)}), bf16[2,8,160,128]{3,0,1,2:T(2,128)(2,1)S(1)}, u32[]{:S(2)}, u32[]{:S(2)}) async-start(bf16[2,8,160,128]{3,0,1,2:T(2,128)(2,1)} %copy.162), calls=%async_computation.8 | async-start | bytes 1310720 | tf_op jit(solution)/shard_map/all_to_all | solution.py:29
  58.3 1.9 fusion.61
  61.7 0.7 constant_dynamic-update-slice_fusion.79
  71.0 0.8 copy-done.10
  71.8 2.2 %fusion.49 = f32[10,128,128]{2,1,0:T(8,128)} fusion(bf16[10,128,128]{1,2,0:T(8,128)(2,1)S(1)} %get-tuple-element.29, bf16[1,16,8,10,128]{4,2,3,1,0:T(8,128)(2,1)} %bitcast.67), kind=kOutput, calls=%fused_computation.93 | convolution fusion | flops 41943040 | bytes 1310720 | tf_op jit(solution)/shard_map/rot,prt->rop/dot_general | solution.py:123
  74.0 7.2 %all-to-all-start.1 = ((bf16[16,1,10,8,128]{4,3,2,1,0:T(8,128)(2,1)}), bf16[16,1,10,8,128]{4,3,2,1,0:T(8,128)(2,1)}, u32[]{:S(2)}, u32[]{:S(2)}) async-start(bf16[16,1,10,8,128]{4,3,2,1,0:T(8,128)(2,1)} %constant_dynamic-update-slice_fusion), calls=%async_computation.1 | async-start | bytes 655360 | tf_op jit(solution)/shard_map/all_to_all | solution.py:16
  81.2 1.3 constant_dynamic-update-slice_fusion.64
  82.6 1.4 fusion.31
  84.0 6.4 %all-to-all-done.1 = bf16[16,1,10,8,128]{4,3,2,1,0:T(8,128)(2,1)} async-done(((bf16[16,1,10,8,128]{4,3,2,1,0:T(8,128)(2,1)}), bf16[16,1,10,8,128]{4,3,2,1,0:T(8,128)(2,1)}, u32[]{:S(2)}, u32[]{:S(2)}) %all-to-all-start.1) | async-done | bytes 327712 | tf_op jit(solution)/shard_map/all_to_all | solution.py:16
  90.3 4.2 %all-to-all-start.10 = ((bf16[16,1,10,8,128]{4,3,2,1,0:T(8,128)(2,1)}), bf16[16,1,10,8,128]{4,3,2,1,0:T(8,128)(2,1)}, u32[]{:S(2)}, u32[]{:S(2)}) async-start(bf16[16,1,10,8,128]{4,3,2,1,0:T(8,128)(2,1)} %constant_dynamic-update-slice_fusion.64), calls=%async_computation.10 | async-start | bytes 655360 | tf_op jit(solution)/shard_map/all_to_all | solution.py:16
  94.5 1.4 constant_dynamic-update-slice_fusion.32
  95.9 1.2 copy.163
  97.1 1.5 convolution_bitcast_fusion
  98.6 5.0 %all-to-all-done.10 = bf16[16,1,10,8,128]{4,3,2,1,0:T(8,128)(2,1)} async-done(((bf16[16,1,10,8,128]{4,3,2,1,0:T(8,128)(2,1)}), bf16[16,1,10,8,128]{4,3,2,1,0:T(8,128)(2,1)}, u32[]{:S(2)}, u32[]{:S(2)}) %all-to-all-start.10) | async-done | bytes 327712 | tf_op jit(solution)/shard_map/all_to_all | solution.py:16
  103.6 4.3 %all-to-all-start.6 = ((bf16[16,2,10,8,128]{4,3,2,1,0:T(8,128)(2,1)}), bf16[16,2,10,8,128]{4,3,2,1,0:T(8,128)(2,1)}, u32[]{:S(2)}, u32[]{:S(2)}) async-start(bf16[16,2,10,8,128]{4,3,2,1,0:T(8,128)(2,1)} %constant_dynamic-update-slice_fusion.32), calls=%async_computation.6 | async-start | bytes 1310720 | tf_op jit(solution)/shard_map/all_to_all | solution.py:16
  107.9 1.3 fusion.24
  109.2 1.9 collective-permute-start
  111.1 2.0 %fusion.53 = f32[8,160,40]{1,2,0:T(8,128)} fusion(bf16[8,40,128]{2,1,0:T(8,128)(2,1)} %bitcast.672, bf16[160,8,128]{2,1,0:T(8,128)(2,1)} %bitcast.169), kind=kOutput, calls=%fused_computation.97 | convolution fusion | flops 13107200 | bytes 614400 | tf_op jit(solution)/shard_map/rpt,pqt->prq/dot_general | solution.py:126
  113.1 1.8 collective-permute-done
  115.3 1.3 copy.133
  116.7 2.0 %all-to-all-done.6 = bf16[16,2,10,8,128]{4,3,2,1,0:T(8,128)(2,1)} async-done(((bf16[16,2,10,8,128]{4,3,2,1,0:T(8,128)(2,1)}), bf16[16,2,10,8,128]{4,3,2,1,0:T(8,128)(2,1)}, u32[]{:S(2)}, u32[]{:S(2)}) %all-to-all-start.6) | async-done | bytes 655392 | tf_op jit(solution)/shard_map/all_to_all | solution.py:16
  118.7 5.3 %all-to-all-start.2 = ((bf16[2,8,160,128]{3,0,1,2:T(2,128)(2,1)}), bf16[2,8,160,128]{3,0,1,2:T(2,128)(2,1)}, u32[]{:S(2)}, u32[]{:S(2)}) async-start(bf16[2,8,160,128]{3,0,1,2:T(2,128)(2,1)} %copy.133), calls=%async_computation.2 | async-start | bytes 1310720 | tf_op jit(solution)/shard_map/all_to_all | solution.py:29
  124.0 1.2 copy.154
  125.5 1.9 collective-permute-start.1
  127.5 1.4 fusion.42
  128.9 0.7 collective-permute-done.1
  129.8 0.9 copy.158
  130.6 8.2 %all-to-all-done.2 = bf16[2,8,160,128]{3,0,1,2:T(2,128)(2,1)} async-done(((bf16[2,8,160,128]{3,0,1,2:T(2,128)(2,1)}), bf16[2,8,160,128]{3,0,1,2:T(2,128)(2,1)}, u32[]{:S(2)}, u32[]{:S(2)}) %all-to-all-start.2) | async-done | bytes 655392 | tf_op jit(solution)/shard_map/all_to_all | solution.py:29
  138.8 4.2 %all-to-all-start.7 = ((bf16[1,8,160,128]{3,1,0,2:T(8,128)(2,1)}), bf16[1,8,160,128]{3,1,0,2:T(8,128)(2,1)}, u32[]{:S(2)}, u32[]{:S(2)}) async-start(bf16[1,8,160,128]{3,1,0,2:T(8,128)(2,1)} %copy.158), calls=%async_computation.7 | async-start | bytes 655360 | tf_op jit(solution)/shard_map/all_to_all | solution.py:29
  143.0 1.2 copy.134
  144.6 0.6 copy-done.1
  155.4 7.1 %all-to-all-start.3 = ((bf16[16,1,10,8,128]{4,3,2,1,0:T(8,128)(2,1)}), bf16[16,1,10,8,128]{4,3,2,1,0:T(8,128)(2,1)}, u32[]{:S(2)}, u32[]{:S(2)}) async-start(bf16[16,1,10,8,128]{4,3,2,1,0:T(8,128)(2,1)} %constant_dynamic-update-slice_fusion.16), calls=%async_computation.3 | async-start | bytes 655360 | tf_op jit(solution)/shard_map/all_to_all | solution.py:16
  162.5 2.1 %fusion.62 = (bf16[1,10,128,128]{2,3,1,0:T(8,128)(2,1)S(1)}, bf16[1,10,128,128]{2,3,1,0:T(8,128)(2,1)S(1)}, bf16[10,128,128]{1,2,0:T(8,128)(2,1)S(1)}) fusion(f32[2,10,128,128]{2,3,1,0:T(8,128)} %convolution_bitcast_fusion, bf16[16,128,128]{2,1,0:T(8,128)(2,1)} %bitcast.653, bf16[1,16,8,10,128]{4,2,3,1,0:T(8,128)(2,1)} %bitcast.107), kind=kOutput, calls=%fused_computation.104 | convolution fusion | flops 44564480 | bytes 2949120 | tf_op jit(solution)/shard_map/prt,rop->rot/dot_general | solution.py:57
  166.7 0.7 copy-done.16
  167.5 4.5 %all-to-all-done.3 = bf16[16,1,10,8,128]{4,3,2,1,0:T(8,128)(2,1)} async-done(((bf16[16,1,10,8,128]{4,3,2,1,0:T(8,128)(2,1)}), bf16[16,1,10,8,128]{4,3,2,1,0:T(8,128)(2,1)}, u32[]{:S(2)}, u32[]{:S(2)}) %all-to-all-start.3) | async-done | bytes 327712 | tf_op jit(solution)/shard_map/all_to_all | solution.py:16
  172.0 4.2 %all-to-all-start.11 = ((bf16[16,1,10,8,128]{4,3,2,1,0:T(8,128)(2,1)}), bf16[16,1,10,8,128]{4,3,2,1,0:T(8,128)(2,1)}, u32[]{:S(2)}, u32[]{:S(2)}) async-start(bf16[16,1,10,8,128]{4,3,2,1,0:T(8,128)(2,1)} %copy-done.16), calls=%async_computation.11 | async-start | bytes 655360 | tf_op jit(solution)/shard_map/all_to_all | solution.py:16
  176.2 0.8 constant_dynamic-update-slice_fusion.48
  177.0 0.9 copy-done.11
  177.8 2.2 %fusion.1 = bf16[2,10,128,128]{3,2,1,0:T(8,128)(2,1)} fusion(f32[2,10,128,128]{3,2,1,0:T(8,128)S(1)} %fusion.31, bf16[2,16,8,10,128]{4,2,3,1,0:T(8,128)(2,1)S(1)} %bitcast.649, bf16[1,10,128,128]{2,3,1,0:T(8,128)(2,1)} %copy-done.21, bf16[1,10,128,128]{2,3,1,0:T(8,128)(2,1)} %copy-done.20), kind=kOutput, calls=%fused_computation.6 | convolution fusion | flops 85196800 | bytes 3276800 | tf_op jit(solution)/shard_map/gprt,grot->grpo/dot_general | solution.py:120
  180.1 5.2 %all-to-all-done.11 = bf16[16,1,10,8,128]{4,3,2,1,0:T(8,128)(2,1)} async-done(((bf16[16,1,10,8,128]{4,3,2,1,0:T(8,128)(2,1)}), bf16[16,1,10,8,128]{4,3,2,1,0:T(8,128)(2,1)}, u32[]{:S(2)}, u32[]{:S(2)}) %all-to-all-start.11) | async-done | bytes 327712 | tf_op jit(solution)/shard_map/all_to_all | solution.py:16
  185.2 3.6 %all-to-all-start.9 = ((bf16[16,2,10,8,128]{4,3,2,1,0:T(8,128)(2,1)}), bf16[16,2,10,8,128]{4,3,2,1,0:T(8,128)(2,1)S(1)}, u32[]{:S(2)}, u32[]{:S(2)}) async-start(bf16[16,2,10,8,128]{4,3,2,1,0:T(8,128)(2,1)} %copy-done.11), calls=%async_computation.9 | async-start | bytes 1310720 | tf_op jit(solution)/shard_map/all_to_all | solution.py:16
  188.8 1.4 fusion.10
  190.4 1.0 reshape.59
  191.4 1.0 reshape.60
  192.3 1.3 fusion.20
  193.9 1.1 reshape.61
  194.9 1.9 add_convert_fusion.1
  196.8 3.1 %all-to-all-done.9 = bf16[16,2,10,8,128]{4,3,2,1,0:T(8,128)(2,1)S(1)} async-done(((bf16[16,2,10,8,128]{4,3,2,1,0:T(8,128)(2,1)}), bf16[16,2,10,8,128]{4,3,2,1,0:T(8,128)(2,1)S(1)}, u32[]{:S(2)}, u32[]{:S(2)}) %all-to-all-start.9) | async-done | bytes 655392 | tf_op jit(solution)/shard_map/all_to_all | solution.py:16
  199.9 1.0 add_convert_fusion
  202.0 0.7 copy.186
  (171 shorter events, 37.6 us)
Async XLA Ops:
  3.3 8.5 %copy-start.26 = (bf16[1,8,6400]{2,1,0:T(8,128)(2,1)S(1)}, bf16[1,8,6400]{2,1,0:T(8,128)(2,1)}, u32[]{:S(2)}) copy-start(bf16[1,8,6400]{2,1,0:T(8,128)(2,1)} %param.17) | copy-start | bytes 307204
  3.3 9.1 %copy-start.14 = (bf16[1,2,10,16384]{3,1,2,0:T(2,128)(2,1)S(1)}, bf16[1,2,10,16384]{3,1,2,0:T(2,128)(2,1)}, u32[]{:S(2)}) copy-start(bf16[1,2,10,16384]{3,1,2,0:T(2,128)(2,1)} %param.15) | copy-start | bytes 1966084
  4.7 8.3 %copy-start.15 = (bf16[1,10,16384]{2,1,0:T(8,128)(2,1)S(1)}, bf16[1,10,16384]{2,1,0:T(8,128)(2,1)}, u32[]{:S(2)}) copy-start(bf16[1,10,16384]{2,1,0:T(8,128)(2,1)} %param.16) | copy-start | bytes 983044
  4.7 20.1 %all-to-all-start = ((bf16[2,8,160,128]{3,0,1,2:T(2,128)(2,1)}), bf16[2,8,160,128]{3,0,1,2:T(2,128)(2,1)S(1)}, u32[]{:S(2)}, u32[]{:S(2)}) async-start(bf16[2,8,160,128]{3,0,1,2:T(2,128)(2,1)} %copy.123), calls=%async_computation | async-start | bytes 1310720 | tf_op jit(solution)/shard_map/all_to_all | solution.py:29
  13.0 48.3 %copy-start = (bf16[2,8,128,128]{3,2,1,0:T(8,128)(2,1)}, bf16[2,8,128,128]{3,2,1,0:T(8,128)(2,1)S(1)}, u32[]{:S(2)}) copy-start(bf16[2,8,128,128]{3,2,1,0:T(8,128)(2,1)S(1)} %copy.217) | copy-start | bytes 1572868
  13.1 3.0 %copy-start.24 = (bf16[1,320,128]{2,1,0:T(8,128)(2,1)S(1)}, bf16[1,320,128]{2,1,0:T(8,128)(2,1)}, u32[]{:S(2)}) copy-start(bf16[1,320,128]{2,1,0:T(8,128)(2,1)} %param.12) | copy-start | bytes 245764
  24.8 15.7 %all-to-all-start.5 = ((bf16[2,8,160,128]{3,0,1,2:T(2,128)(2,1)}), bf16[2,8,160,128]{3,0,1,2:T(2,128)(2,1)S(1)}, u32[]{:S(2)}, u32[]{:S(2)}) async-start(bf16[2,8,160,128]{3,0,1,2:T(2,128)(2,1)} %copy.147), calls=%async_computation.5 | async-start | bytes 1310720 | tf_op jit(solution)/shard_map/all_to_all | solution.py:29
  40.5 14.2 %all-to-all-start.4 = ((bf16[1,8,160,128]{3,1,0,2:T(8,128)(2,1)}), bf16[1,8,160,128]{3,1,0,2:T(8,128)(2,1)}, u32[]{:S(2)}, u32[]{:S(2)}) async-start(bf16[1,8,160,128]{3,1,0,2:T(8,128)(2,1)} %copy.143), calls=%async_computation.4 | async-start | bytes 655360 | tf_op jit(solution)/shard_map/all_to_all | solution.py:29
  54.7 19.3 %all-to-all-start.8 = ((bf16[2,8,160,128]{3,0,1,2:T(2,128)(2,1)}), bf16[2,8,160,128]{3,0,1,2:T(2,128)(2,1)S(1)}, u32[]{:S(2)}, u32[]{:S(2)}) async-start(bf16[2,8,160,128]{3,0,1,2:T(2,128)(2,1)} %copy.162), calls=%async_computation.8 | async-start | bytes 1310720 | tf_op jit(solution)/shard_map/all_to_all | solution.py:29
  60.3 0.8 copy-start.22
  60.3 0.8 copy-start.23
  60.9 10.0 %copy-start.12 = (bf16[2,10,128,128]{3,2,1,0:T(8,128)(2,1)}, bf16[2,10,128,128]{3,2,1,0:T(8,128)(2,1)S(1)}, u32[]{:S(2)}) copy-start(bf16[2,10,128,128]{3,2,1,0:T(8,128)(2,1)S(1)} %fusion.2) | copy-start | bytes 1966084
  61.7 9.2 %copy-start.9 = (bf16[1,10,128,128]{3,2,1,0:T(8,128)(2,1)}, bf16[1,10,128,128]{3,2,1,0:T(8,128)(2,1)S(1)}, u32[]{:S(2)}) copy-start(bf16[1,10,128,128]{3,2,1,0:T(8,128)(2,1)S(1)} %fusion.14) | copy-start | bytes 983044
  71.0 0.8 copy-start.10
  74.0 7.2 %copy-start.5 = (bf16[2,8,160,128]{3,0,1,2:T(2,128)(2,1)}, bf16[2,8,160,128]{3,0,1,2:T(2,128)(2,1)S(1)}, u32[]{:S(2)}) copy-start(bf16[2,8,160,128]{3,0,1,2:T(2,128)(2,1)S(1)} %all-to-all-done.8) | copy-start | bytes 1966084
  74.0 16.3 %all-to-all-start.1 = ((bf16[16,1,10,8,128]{4,3,2,1,0:T(8,128)(2,1)}), bf16[16,1,10,8,128]{4,3,2,1,0:T(8,128)(2,1)}, u32[]{:S(2)}, u32[]{:S(2)}) async-start(bf16[16,1,10,8,128]{4,3,2,1,0:T(8,128)(2,1)} %constant_dynamic-update-slice_fusion), calls=%async_computation.1 | async-start | bytes 655360 | tf_op jit(solution)/shard_map/all_to_all | solution.py:16
  90.3 13.3 %all-to-all-start.10 = ((bf16[16,1,10,8,128]{4,3,2,1,0:T(8,128)(2,1)}), bf16[16,1,10,8,128]{4,3,2,1,0:T(8,128)(2,1)}, u32[]{:S(2)}, u32[]{:S(2)}) async-start(bf16[16,1,10,8,128]{4,3,2,1,0:T(8,128)(2,1)} %constant_dynamic-update-slice_fusion.64), calls=%async_computation.10 | async-start | bytes 655360 | tf_op jit(solution)/shard_map/all_to_all | solution.py:16
  98.6 9.3 %copy-start.17 = (bf16[1,320,128]{2,1,0:T(8,128)(2,1)S(1)}, bf16[1,320,128]{2,1,0:T(8,128)(2,1)}, u32[]{:S(2)}) copy-start(bf16[1,320,128]{2,1,0:T(8,128)(2,1)} %param.9) | copy-start | bytes 245764
  103.6 15.1 %all-to-all-start.6 = ((bf16[16,2,10,8,128]{4,3,2,1,0:T(8,128)(2,1)}), bf16[16,2,10,8,128]{4,3,2,1,0:T(8,128)(2,1)}, u32[]{:S(2)}, u32[]{:S(2)}) async-start(bf16[16,2,10,8,128]{4,3,2,1,0:T(8,128)(2,1)} %constant_dynamic-update-slice_fusion.32), calls=%async_computation.6 | async-start | bytes 1310720 | tf_op jit(solution)/shard_map/all_to_all | solution.py:16
  107.9 7.1 %copy-start.18 = (bf16[320,128]{1,0:T(8,128)(2,1)S(1)}, bf16[320,128]{1,0:T(8,128)(2,1)}, u32[]{:S(2)}) copy-start(bf16[320,128]{1,0:T(8,128)(2,1)} %param.10) | copy-start | bytes 245764
  109.2 5.8 %collective-permute-start = (bf16[8,40,128]{2,1,0:T(8,128)(2,1)S(1)}, bf16[8,40,128]{2,1,0:T(8,128)(2,1)S(1)}, u32[]{:S(2)}, u32[]{:S(2)}) collective-permute-start(bf16[8,40,128]{2,1,0:T(8,128)(2,1)S(1)} %fusion.24), channel_id=1, source_target_pairs={{0,16},{16,32},{32,48},{48,64},{64,80},{80,96},{96,112},{112,128},... | collective-permute-start | bytes 245768 | tf_op jit(solution)/shard_map/ppermute | solution.py:25
  118.7 20.1 %all-to-all-start.2 = ((bf16[2,8,160,128]{3,0,1,2:T(2,128)(2,1)}), bf16[2,8,160,128]{3,0,1,2:T(2,128)(2,1)}, u32[]{:S(2)}, u32[]{:S(2)}) async-start(bf16[2,8,160,128]{3,0,1,2:T(2,128)(2,1)} %copy.133), calls=%async_computation.2 | async-start | bytes 1310720 | tf_op jit(solution)/shard_map/all_to_all | solution.py:29
  124.0 1.2 copy-start.25
  125.2 4.3 %copy-start.27 = (bf16[320,128]{1,0:T(8,128)(2,1)S(1)}, bf16[320,128]{1,0:T(8,128)(2,1)}, u32[]{:S(2)}) copy-start(bf16[320,128]{1,0:T(8,128)(2,1)} %param.13) | copy-start | bytes 245764
  125.5 4.0 %collective-permute-start.1 = (bf16[8,40,128]{2,1,0:T(8,128)(2,1)S(1)}, bf16[8,40,128]{2,1,0:T(8,128)(2,1)S(1)}, u32[]{:S(2)}, u32[]{:S(2)}) collective-permute-start(bf16[8,40,128]{2,1,0:T(8,128)(2,1)S(1)} %fusion.23), channel_id=1, source_target_pairs={{16,0},{32,16},{48,32},{64,48},{80,64},{96,80},{112,96},{128,112},... | collective-permute-start | bytes 245768 | tf_op jit(solution)/shard_map/ppermute | solution.py:25
  138.8 16.5 %all-to-all-start.7 = ((bf16[1,8,160,128]{3,1,0,2:T(8,128)(2,1)}), bf16[1,8,160,128]{3,1,0,2:T(8,128)(2,1)}, u32[]{:S(2)}, u32[]{:S(2)}) async-start(bf16[1,8,160,128]{3,1,0,2:T(8,128)(2,1)} %copy.158), calls=%async_computation.7 | async-start | bytes 655360 | tf_op jit(solution)/shard_map/all_to_all | solution.py:29
  144.2 1.0 copy-start.1
  155.4 16.6 %all-to-all-start.3 = ((bf16[16,1,10,8,128]{4,3,2,1,0:T(8,128)(2,1)}), bf16[16,1,10,8,128]{4,3,2,1,0:T(8,128)(2,1)}, u32[]{:S(2)}, u32[]{:S(2)}) async-start(bf16[16,1,10,8,128]{4,3,2,1,0:T(8,128)(2,1)} %constant_dynamic-update-slice_fusion.16), calls=%async_computation.3 | async-start | bytes 655360 | tf_op jit(solution)/shard_map/all_to_all | solution.py:16
  164.6 0.8 copy-start.20
  164.6 0.9 copy-start.21
  164.6 1.1 copy-start.8
  164.6 1.4 copy-start.2
  165.2 1.5 copy-start.13
  166.7 0.7 copy-start.16
  172.0 13.3 %all-to-all-start.11 = ((bf16[16,1,10,8,128]{4,3,2,1,0:T(8,128)(2,1)}), bf16[16,1,10,8,128]{4,3,2,1,0:T(8,128)(2,1)}, u32[]{:S(2)}, u32[]{:S(2)}) async-start(bf16[16,1,10,8,128]{4,3,2,1,0:T(8,128)(2,1)} %copy-done.16), calls=%async_computation.11 | async-start | bytes 655360 | tf_op jit(solution)/shard_map/all_to_all | solution.py:16
  177.0 0.9 copy-start.11
  180.1 8.8 %copy-start.3 = (f32[10,128,128]{2,1,0:T(8,128)S(1)}, f32[10,128,128]{2,1,0:T(8,128)}, u32[]{:S(2)}) copy-start(f32[10,128,128]{2,1,0:T(8,128)} %fusion.49) | copy-start | bytes 1966084
  180.1 10.2 %copy-start.6 = (bf16[2,10,128,128]{3,2,1,0:T(8,128)(2,1)S(1)}, bf16[2,10,128,128]{3,2,1,0:T(8,128)(2,1)}, u32[]{:S(2)}) copy-start(bf16[2,10,128,128]{3,2,1,0:T(8,128)(2,1)} %fusion.1) | copy-start | bytes 1966084
  185.2 14.6 %all-to-all-start.9 = ((bf16[16,2,10,8,128]{4,3,2,1,0:T(8,128)(2,1)}), bf16[16,2,10,8,128]{4,3,2,1,0:T(8,128)(2,1)S(1)}, u32[]{:S(2)}, u32[]{:S(2)}) async-start(bf16[16,2,10,8,128]{4,3,2,1,0:T(8,128)(2,1)} %copy-done.11), calls=%async_computation.9 | async-start | bytes 1310720 | tf_op jit(solution)/shard_map/all_to_all | solution.py:16
  190.4 2.0 copy-start.7
  191.4 3.5 %copy-start.19 = (bf16[320,128]{1,0:T(8,128)(2,1)S(1)}, bf16[320,128]{1,0:T(8,128)(2,1)}, u32[]{:S(2)}) copy-start(bf16[320,128]{1,0:T(8,128)(2,1)} %param.10) | copy-start | bytes 245764
  199.9 1.1 copy-start.4
